TPU v7x, 32 devices: a whole 2x2x4 slice. The times are simulated.
32 devices in a mesh: sector: 8 (over y, x, core), sub: 4 (over z).
Axes of the slice: x: 2, y: 2, z: 4, core: 2. Of those that a mesh axis runs over, the one named last changes fastest.
Arguments:
- dual_load: float32 [8, 4, 2, 512, 256], P('sector', 'sub'), may hold values from -50 to 50
- flexibility: bfloat16 [8, 4, 2048, 2048], P('sector', 'sub'), may hold values from -10 to 10, as said below
- face_order: int32 [8, 4, 2048], P('sector', 'sub'), may hold values from 0 to 2047, each once within a row
- corner_index: int32 [8, 4, 32], P('sector', 'sub'), may hold values from 0 to 2047, as said below
- coarse_inverse: float32 [256, 256], replicated, may hold values from -10 to 10, as said below
Outputs:
- multiplier: float32 [8, 4, 2, 512, 256], P('sector', 'sub')
- residual: float32 [8, 4, 2, 512, 256], P('sector', 'sub')
Inputs may be any that keep to these rules, and one draw needn't show every extreme that they name: `flexibility`: a block of sizes of order one with a dominant diagonal; each subdomain's matrix is symmetric positive definite. `corner_index`: entries within one subdomain are distinct. `face_order`: each subdomain's row names every face slot once. `coarse_inverse`: symmetric positive definite with a dominant diagonal.
All inputs are finite; a program needn't handle non-finite values.
Results may differ from a plain program's by a relative error of at most 0.0087.
The roundings to bfloat16 on the way count: a program that leaves them out, or rounds other values in their place, can miss the bound.
Values may be sent and summed in bfloat16 or wider, within the bound.
No kernel may reach another device: no remote copies, remote signals or barrier semaphores. Data moves between devices by JAX's collectives and lax.ppermute only.
A program may use at most 128 MiB of HBM per device.

v0:
```python
import jax
import jax.numpy as jnp
from jax import lax
from jax.sharding import PartitionSpec as P

ITERS = 2


def passed_along(x, axis, by):
    count = lax.axis_size(axis)
    pairs = [(i, i + by) for i in range(count) if 0 <= i + by < count]
    return lax.ppermute(x, axis, pairs)


def from_behind(value, axis, steps):
    count = lax.axis_size(axis)
    pairs = [(source, (source + steps) % count) for source in range(count)]
    return lax.ppermute(value, axis, pairs)


def squares(residual):
    return lax.psum(jnp.sum(residual * residual, axis=(0, 1, 2, 3)), ("sector", "sub"))


def inner_sum(left, right):
    return jnp.sum(left * right, axis=(0, 1, 2, 3))


def shards(dual_load, flexibility, face_order, corner_index, coarse_inverse):
    slot_order = face_order[0, 0]
    corners = corner_index[0, 0]
    corner_count = corners.shape[0]
    matrix = jnp.take(jnp.take(flexibility[0, 0], slot_order, axis=0), slot_order, axis=1)
    face_width = slot_order.shape[0] // 4
    cases = dual_load.shape[-1]
    sub_count = lax.axis_size("sub")
    multiplier = jnp.zeros_like(dual_load)
    residual = dual_load
    direction = dual_load
    norm_now = squares(residual)
    for iteration in range(ITERS):
        rounded = direction[0, 0].astype(jnp.bfloat16)
        lower_sub = passed_along(rounded[0], "sub", 1)
        previous = from_behind(rounded[1], "sector", 1)
        face_stack = jnp.concatenate([-lower_sub, rounded[0], -previous, rounded[1]], axis=0)
        partial_value = jnp.take(face_stack, corners, axis=0).astype(jnp.float32)
        sector_total = lax.psum(partial_value.astype(jnp.bfloat16), "sub").astype(jnp.float32)
        sector_id = lax.axis_index("sector")
        everything = lax.all_gather(sector_total, "sector", axis=0, tiled=True)
        inverse_rows = lax.dynamic_slice_in_dim(
            coarse_inverse, sector_id * corner_count, corner_count, 0
        )
        coarse = jnp.dot(
            inverse_rows,
            everything,
            precision=lax.Precision.HIGHEST,
            preferred_element_type=jnp.float32,
        )
        coarse = coarse / sub_count
        correction = jnp.zeros((4 * face_width, cases), jnp.float32).at[corners].add(coarse)
        product = jnp.dot(matrix, face_stack, preferred_element_type=jnp.float32) + correction
        outgoing_sub = product[:face_width]
        outgoing_cycle = product[2 * face_width : 3 * face_width]
        upper_next = passed_along(outgoing_sub.astype(jnp.bfloat16), "sub", -1)
        cycle_next = from_behind(outgoing_cycle.astype(jnp.bfloat16), "sector", -1)
        own_sub = product[face_width : 2 * face_width]
        own_cycle = product[3 * face_width :]
        jump_pair = jnp.stack(
            [own_sub - upper_next.astype(jnp.float32), own_cycle - cycle_next.astype(jnp.float32)],
            axis=0,
        )
        image = jump_pair[None, None]
        curvature = lax.psum(inner_sum(direction, image), ("sector", "sub"))
        alpha = norm_now / curvature
        multiplier = multiplier + alpha * direction
        residual = residual - alpha * image
        if iteration + 1 < ITERS:
            norm_next = squares(residual)
            direction = residual + norm_next / norm_now * direction
            norm_now = norm_next
    return (multiplier, residual)


def solution(mesh):
    return jax.shard_map(
        shards,
        mesh=mesh,
        in_specs=(
            P("sector", "sub", None, None, None),
            P("sector", "sub", None, None),
            P("sector", "sub", None),
            P("sector", "sub", None),
            P(),
        ),
        out_specs=(P("sector", "sub", None, None, None), P("sector", "sub", None, None, None)),
        check_vma=False,
    )
```

profile of v0, /device:TPU:10, one launch (start us, length us, event | category | flops | bytes accessed | tf_op | source)
XLA Modules:
  0.0 299.7 jit_solution(9664023918029677284)
XLA Ops:
  2.1 3.5 %collective-permute-start = (bf16[512,256]{1,0:T(8,128)(2,1)S(1)}, bf16[512,256]{1,0:T(8,128)(2,1)S(1)}, u32[]{:S(2)}, u32[]{:S(2)}) collective-permute-start(bf16[512,256]{1,0:T(8,128)(2,1)S(1)} %get-tuple-element.27), channel_id=1, source_target_pairs={{0,1},{1,2},{2,3},{4,5},{5,6},{6,7},{8,9},{9,10},{10,11},{12,13},{... | collective-permute-start | bytes 786440 | tf_op jit(solution)/shard_map/ppermute | solution.py:12
  5.7 20.8 %gather_fusion = bf16[2048,2048]{1,0:T(8,128)(2,1)} fusion(bf16[2048,2048]{1,0:T(8,128)(2,1)} %bitcast.51, s32[2048]{0:T(1024)S(1)} %broadcast_clamp_fusion), kind=kCustom, calls=%fused_computation.2 | custom fusion | bytes 16785408 | tf_op jit(solution)/shard_map/jit(_take)/gather | solution.py:33
  26.5 7.4 %broadcast_select_fusion = bf16[2048,2048]{1,0:T(8,128)(2,1)} fusion(bf16[2048,2048]{1,0:T(8,128)(2,1)} %gather_fusion, pred[2048]{0:T(1024)(128)(4,1)S(1)} %compare_and_fusion), kind=kLoop, calls=%fused_computation.6 | loop fusion | flops 4194304 | bytes 16779264 | tf_op jit(solution)/shard_map/jit(_take)/select_n | solution.py:33
  33.9 12.3 %copy.8 = bf16[2048,2048]{0,1:T(8,128)(2,1)} copy(bf16[2048,2048]{1,0:T(8,128)(2,1)} %broadcast_select_fusion) | data formatting | bytes 16777216 | tf_op jit(solution)/shard_map/jit(_take)/select_n | solution.py:33
  46.3 20.8 %gather_fusion.1 = bf16[2048,2048]{1,0:T(8,128)(2,1)} fusion(bf16[2048,2048]{0,1:T(8,128)(2,1)} %copy.8, s32[2048]{0:T(1024)S(1)} %broadcast_clamp_fusion), kind=kCustom, calls=%fused_computation.3 | custom fusion | bytes 16785408 | tf_op jit(solution)/shard_map/jit(_take)/gather | solution.py:33
  67.3 6.5 %fusion = f32[2048,256]{1,0:T(8,128)S(1)} fusion(bf16[2048,2048]{1,0:T(8,128)(2,1)} %gather_fusion.1, pred[2048]{0:T(1024)(128)(4,1)S(1)} %compare_and_fusion, bf16[512,256]{1,0:T(8,128)(2,1)} %copy-done.5, bf16[512,256]{1,0:T(8,128)(2,1)S(1)} %neg.13, bf16[512,256]{1,0:T(8,128)(2,1)} %copy-done.4, bf16[512,256]{1,0:T(8,128)(2,1)S(1)} %neg.12), kind=kOutput, calls=%fused_computation.8 | convolution fusion | flops 2155872256 | bytes 11536384 | tf_op jit(solution)/shard_map/dot_general | solution.py:61
  74.5 14.2 %psum.43 = bf16[32,256]{1,0:T(8,128)(2,1)S(1)} all-reduce(bf16[32,256]{1,0:T(8,128)(2,1)S(1)} %broadcast_select_fusion.5), channel_id=1, replica_groups=mesh['sector'=8,'sub'=4] {'sub'}, use_global_device_ids=true, to_apply=%region_2.4 | all-reduce | flops 8192 | bytes 32768 | tf_op jit(solution)/shard_map/psum | solution.py:47
  88.7 9.3 %all_gather.6 = f32[256,256]{1,0:T(8,128)S(1)} all-gather(f32[32,256]{1,0:T(8,128)S(1)} %convert_element_type.35), channel_id=1, replica_groups=mesh['sector'=8,'sub'=4] {'sector'}, dimensions={0}, use_global_device_ids=true | all-gather | bytes 294912 | tf_op jit(solution)/shard_map/all_gather | solution.py:49
  101.2 5.2 %collective-permute-start.2 = (bf16[512,256]{1,0:T(8,128)(2,1)S(1)}, bf16[512,256]{1,0:T(8,128)(2,1)S(1)}, u32[]{:S(2)}, u32[]{:S(2)}) collective-permute-start(bf16[512,256]{1,0:T(8,128)(2,1)S(1)} %get-tuple-element.23), channel_id=1, source_target_pairs={{1,0},{2,1},{3,2},{5,4},{6,5},{7,6},{9,8},{10,9},{11,10},{13,12},{... | collective-permute-start | bytes 786440 | tf_op jit(solution)/shard_map/ppermute | solution.py:12
  106.7 5.8 %collective-permute-done.2 = bf16[512,256]{1,0:T(8,128)(2,1)S(1)} collective-permute-done((bf16[512,256]{1,0:T(8,128)(2,1)S(1)}, bf16[512,256]{1,0:T(8,128)(2,1)S(1)}, u32[]{:S(2)}, u32[]{:S(2)}) %collective-permute-start.2) | collective-permute-done | bytes 262176 | tf_op jit(solution)/shard_map/ppermute | solution.py:12
  114.1 41.2 %all-reduce = (f32[256]{0:T(256)S(1)}, f32[256]{0:T(256)S(1)}) all-reduce(f32[256]{0:T(256)S(1)} %get-tuple-element.4, f32[256]{0:T(256)S(1)} %get-tuple-element.3), channel_id=1, replica_groups=mesh['sector'=8,'sub'=4] {'sector','sub'}, use_global_device_ids=true, to_apply=%region_1.2 | all-reduce | flops 512 | bytes 4096 | tf_op jit(solution)/shard_map/psum | solution.py:22
  155.5 39.3 %psum.45 = f32[256]{0:T(256)S(1)} all-reduce(f32[256]{0:T(256)S(1)} %multiply_reduce_fusion), channel_id=1, replica_groups=mesh['sector'=8,'sub'=4] {'sector','sub'}, use_global_device_ids=true, to_apply=%region_7.9 | all-reduce | flops 256 | bytes 2048 | tf_op jit(solution)/shard_map/psum | solution.py:22
  195.1 2.6 collective-permute-start.4
  197.7 3.2 %collective-permute-done.5 = bf16[512,256]{1,0:T(8,128)(2,1)S(1)} collective-permute-done((bf16[512,256]{1,0:T(8,128)(2,1)S(1)}, bf16[512,256]{1,0:T(8,128)(2,1)S(1)}, u32[]{:S(2)}, u32[]{:S(2)}) %collective-permute-start.5) | collective-permute-done | bytes 262176 | tf_op jit(solution)/shard_map/ppermute | solution.py:18
  201.0 4.7 %collective-permute-done.4 = bf16[512,256]{1,0:T(8,128)(2,1)S(1)} collective-permute-done((bf16[512,256]{1,0:T(8,128)(2,1)S(1)}, bf16[512,256]{1,0:T(8,128)(2,1)S(1)}, u32[]{:S(2)}, u32[]{:S(2)}) %collective-permute-start.4) | collective-permute-done | bytes 262176 | tf_op jit(solution)/shard_map/ppermute | solution.py:12
  205.7 7.8 %fusion.1 = f32[2048,256]{1,0:T(8,128)} fusion(bf16[2048,2048]{1,0:T(8,128)(2,1)} %gather_fusion.1, pred[2048]{0:T(1024)(128)(4,1)S(1)} %compare_and_fusion, bf16[512,256]{1,0:T(8,128)(2,1)S(1)} %get-tuple-element.26, bf16[512,256]{1,0:T(8,128)(2,1)S(1)} %neg.15, bf16[512,256]{1,0:T(8,128)(2,1)S(1)} %get-tuple-element.25, bf16[512,256]{1,0:T(8,128)(2,1)S(1)} %neg.14), kind=kOutput, calls=%fused_computation.9 | convolution fusion | flops 2155872256 | bytes 11536384 | tf_op jit(solution)/shard_map/dot_general | solution.py:61
  214.3 14.9 %psum.46 = bf16[32,256]{1,0:T(8,128)(2,1)S(1)} all-reduce(bf16[32,256]{1,0:T(8,128)(2,1)S(1)} %broadcast_select_fusion.4), channel_id=1, replica_groups=mesh['sector'=8,'sub'=4] {'sub'}, use_global_device_ids=true, to_apply=%region_8.10 | all-reduce | flops 8192 | bytes 32768 | tf_op jit(solution)/shard_map/psum | solution.py:47
  229.2 8.8 %all_gather.7 = f32[256,256]{1,0:T(8,128)S(1)} all-gather(f32[32,256]{1,0:T(8,128)S(1)} %convert_element_type.39), channel_id=1, replica_groups=mesh['sector'=8,'sub'=4] {'sector'}, dimensions={0}, use_global_device_ids=true | all-gather | bytes 294912 | tf_op jit(solution)/shard_map/all_gather | solution.py:49
  238.2 3.7 %scatter_fusion.1 = f32[2048,256]{1,0:T(8,128)} fusion(f32[2048,256]{1,0:T(8,128)} %fusion.1, s32[32]{0:T(128)S(1)} %fusion.19, f32[32,256]{1,0:T(8,128)S(1)} %convolution_multiply_fusion), kind=kCustom, calls=%fused_computation.5 | custom fusion | flops 8192 | bytes 98432 | tf_op jit(solution)/shard_map/scatter-add | solution.py:60
  241.9 1.8 convert.9
  243.8 6.0 %collective-permute-start.6 = (bf16[512,256]{1,0:T(8,128)(2,1)S(1)}, bf16[512,256]{1,0:T(8,128)(2,1)S(1)}, u32[]{:S(2)}, u32[]{:S(2)}) collective-permute-start(bf16[512,256]{1,0:T(8,128)(2,1)S(1)} %get-tuple-element.21), channel_id=1, source_target_pairs={{1,0},{2,1},{3,2},{5,4},{6,5},{7,6},{9,8},{10,9},{11,10},{13,12},{... | collective-permute-start | bytes 786440 | tf_op jit(solution)/shard_map/ppermute | solution.py:12
  250.9 4.9 %collective-permute-done.6 = bf16[512,256]{1,0:T(8,128)(2,1)S(1)} collective-permute-done((bf16[512,256]{1,0:T(8,128)(2,1)S(1)}, bf16[512,256]{1,0:T(8,128)(2,1)S(1)}, u32[]{:S(2)}, u32[]{:S(2)}) %collective-permute-start.6) | collective-permute-done | bytes 262176 | tf_op jit(solution)/shard_map/ppermute | solution.py:12
  256.3 41.8 %psum.47 = f32[256]{0:T(256)S(1)} all-reduce(f32[256]{0:T(256)S(1)} %fusion.6), channel_id=1, replica_groups=mesh['sector'=8,'sub'=4] {'sector','sub'}, use_global_device_ids=true, to_apply=%region_11.13 | all-reduce | flops 256 | bytes 2048 | tf_op jit(solution)/shard_map/psum | solution.py:73
  298.1 1.6 fusion.7
  (61 shorter events, 10.6 us)
Async XLA Ops:
  0.6 97.4 %copy-start = (f32[256,256]{1,0:T(8,128)S(1)}, f32[256,256]{1,0:T(8,128)}, u32[]{:S(2)}) copy-start(f32[256,256]{1,0:T(8,128)} %param.11) | copy-start | bytes 786436
  0.6 5.0 %copy-start.7 = (s32[1,1,32]{2,1,0:T(1,128)S(1)}, s32[1,1,32]{2,1,0:T(1,128)}, u32[]{:S(2)}) copy-start(s32[1,1,32]{2,1,0:T(1,128)} %param.10) | copy-start | bytes 388
  0.7 5.0 %copy-start.6 = (s32[1,1,2048]{2,1,0:T(1,128)S(1)}, s32[1,1,2048]{2,1,0:T(1,128)}, u32[]{:S(2)}) copy-start(s32[1,1,2048]{2,1,0:T(1,128)} %param.9) | copy-start | bytes 24580
  2.0 65.2 %copy-start.4 = (bf16[512,256]{1,0:T(8,128)(2,1)}, bf16[512,256]{1,0:T(8,128)(2,1)S(1)}, u32[]{:S(2)}) copy-start(bf16[512,256]{1,0:T(8,128)(2,1)S(1)} %get-tuple-element.27) | copy-start | bytes 786436
  2.0 65.2 %copy-start.5 = (bf16[512,256]{1,0:T(8,128)(2,1)}, bf16[512,256]{1,0:T(8,128)(2,1)S(1)}, u32[]{:S(2)}) copy-start(bf16[512,256]{1,0:T(8,128)(2,1)S(1)} %get-tuple-element.28) | copy-start | bytes 786436
  2.1 65.0 %collective-permute-start.1 = (bf16[512,256]{1,0:T(8,128)(2,1)S(1)}, bf16[512,256]{1,0:T(8,128)(2,1)S(1)}, u32[]{:S(2)}, u32[]{:S(2)}) collective-permute-start(bf16[512,256]{1,0:T(8,128)(2,1)S(1)} %get-tuple-element.28), channel_id=1, source_target_pairs={{0,4},{4,8},{8,12},{12,16},{16,20},{20,24},{24,28},{28,0},{1,5},{5... | collective-permute-start | bytes 786440 | tf_op jit(solution)/shard_map/ppermute | solution.py:18
  2.1 65.0 %collective-permute-start = (bf16[512,256]{1,0:T(8,128)(2,1)S(1)}, bf16[512,256]{1,0:T(8,128)(2,1)S(1)}, u32[]{:S(2)}, u32[]{:S(2)}) collective-permute-start(bf16[512,256]{1,0:T(8,128)(2,1)S(1)} %get-tuple-element.27), channel_id=1, source_target_pairs={{0,1},{1,2},{2,3},{4,5},{5,6},{6,7},{8,9},{9,10},{10,11},{12,13},{... | collective-permute-start | bytes 786440 | tf_op jit(solution)/shard_map/ppermute | solution.py:12
  99.8 1.4 copy-start.3
  101.2 12.6 %copy-start.1 = (f32[1,1,2,512,256]{4,3,2,1,0:T(8,128)S(1)}, f32[1,1,2,512,256]{4,3,2,1,0:T(8,128)}, u32[]{:S(2)}) copy-start(f32[1,1,2,512,256]{4,3,2,1,0:T(8,128)} %param.7) | copy-start | bytes 3145732
  101.2 11.3 %collective-permute-start.2 = (bf16[512,256]{1,0:T(8,128)(2,1)S(1)}, bf16[512,256]{1,0:T(8,128)(2,1)S(1)}, u32[]{:S(2)}, u32[]{:S(2)}) collective-permute-start(bf16[512,256]{1,0:T(8,128)(2,1)S(1)} %get-tuple-element.23), channel_id=1, source_target_pairs={{1,0},{2,1},{3,2},{5,4},{6,5},{7,6},{9,8},{10,9},{11,10},{13,12},{... | collective-permute-start | bytes 786440 | tf_op jit(solution)/shard_map/ppermute | solution.py:12
  106.4 6.1 %collective-permute-start.3 = (bf16[512,256]{1,0:T(8,128)(2,1)S(1)}, bf16[512,256]{1,0:T(8,128)(2,1)S(1)}, u32[]{:S(2)}, u32[]{:S(2)}) collective-permute-start(bf16[512,256]{1,0:T(8,128)(2,1)S(1)} %get-tuple-element.24), channel_id=1, source_target_pairs={{0,28},{4,0},{8,4},{12,8},{16,12},{20,16},{24,20},{28,24},{1,29},{... | collective-permute-start | bytes 786440 | tf_op jit(solution)/shard_map/ppermute | solution.py:18
  195.1 5.8 %collective-permute-start.5 = (bf16[512,256]{1,0:T(8,128)(2,1)S(1)}, bf16[512,256]{1,0:T(8,128)(2,1)S(1)}, u32[]{:S(2)}, u32[]{:S(2)}) collective-permute-start(bf16[512,256]{1,0:T(8,128)(2,1)S(1)} %get-tuple-element.26), channel_id=1, source_target_pairs={{0,4},{4,8},{8,12},{12,16},{16,20},{20,24},{24,28},{28,0},{1,5},{5... | collective-permute-start | bytes 786440 | tf_op jit(solution)/shard_map/ppermute | solution.py:18
  195.1 10.5 %collective-permute-start.4 = (bf16[512,256]{1,0:T(8,128)(2,1)S(1)}, bf16[512,256]{1,0:T(8,128)(2,1)S(1)}, u32[]{:S(2)}, u32[]{:S(2)}) collective-permute-start(bf16[512,256]{1,0:T(8,128)(2,1)S(1)} %get-tuple-element.25), channel_id=1, source_target_pairs={{0,1},{1,2},{2,3},{4,5},{5,6},{6,7},{8,9},{9,10},{10,11},{12,13},{... | collective-permute-start | bytes 786440 | tf_op jit(solution)/shard_map/ppermute | solution.py:12
  241.9 14.0 %copy-start.2 = (f32[2048,256]{1,0:T(8,128)S(1)}, f32[2048,256]{1,0:T(8,128)}, u32[]{:S(2)}) copy-start(f32[2048,256]{1,0:T(8,128)} %scatter_fusion.1) | copy-start | bytes 6291460
  243.8 12.1 %collective-permute-start.6 = (bf16[512,256]{1,0:T(8,128)(2,1)S(1)}, bf16[512,256]{1,0:T(8,128)(2,1)S(1)}, u32[]{:S(2)}, u32[]{:S(2)}) collective-permute-start(bf16[512,256]{1,0:T(8,128)(2,1)S(1)} %get-tuple-element.21), channel_id=1, source_target_pairs={{1,0},{2,1},{3,2},{5,4},{6,5},{7,6},{9,8},{10,9},{11,10},{13,12},{... | collective-permute-start | bytes 786440 | tf_op jit(solution)/shard_map/ppermute | solution.py:12
  249.8 6.1 %collective-permute-start.7 = (bf16[512,256]{1,0:T(8,128)(2,1)S(1)}, bf16[512,256]{1,0:T(8,128)(2,1)S(1)}, u32[]{:S(2)}, u32[]{:S(2)}) collective-permute-start(bf16[512,256]{1,0:T(8,128)(2,1)S(1)} %get-tuple-element.22), channel_id=1, source_target_pairs={{0,28},{4,0},{8,4},{12,8},{16,12},{20,16},{24,20},{28,24},{1,29},{... | collective-permute-start | bytes 786440 | tf_op jit(solution)/shard_map/ppermute | solution.py:18
where the time goes:
time: 301 us; the launch traced here: 300 us
  blocking collectives  170 us (56%)
  local copies, waits for them, and re-layouts  56.6 us (19%)
  other arithmetic  20.5 us (7%)
  starting transfers between devices  18.8 us (6%)
  waiting for transfers between devices  18.6 us (6%)
  matrix products  14.8 us (5%)
    psum x2, blocking collectives, squares(): lax.psum(jnp.sum(residual * residual, axis=(0, 1, 2, 3)), ('sector', 'sub'))  80.5 us
    psum x1, blocking collectives, shards(): curvature = lax.psum(inner_sum(direction, image), ('sector', 'sub'))  41.8 us
    psum x2, blocking collectives, shards(): lax.psum(partial_value.astype(jnp.bfloat16), 'sub').astype(jnp.float32)  29.2 us
    gather x1, local copies, waits for them, and re-layouts, shards(): jnp.take(flexibility[0, 0], slot_order, axis=0)  20.8 us
    gather x1, local copies, waits for them, and re-layouts, shards(): jnp.take(jnp.take(flexibility[0, 0], slot_order, axis=0), slot_order, axi...  20.8 us
    all_gather x2, blocking collectives, shards(): everything = lax.all_gather(sector_total, 'sector', axis=0, tiled=True)  18.1 us
    ppermute x4, starting transfers between devices, passed_along(): return lax.ppermute(x, axis, pairs)  17.2 us
    ppermute x4, waiting for transfers between devices, passed_along(): return lax.ppermute(x, axis, pairs)  15.4 us
  transfers between devices with their start and end apart: 8, of which 4 were waited for; matrix products, arithmetic and copies ran while one was open for 21% of the time, Pallas kernels for 0%

commit v1 on v0

--- a/solution.py
+++ b/solution.py
@@ -4,6 +4,19 @@
 from jax.sharding import PartitionSpec as P
 
 ITERS = 2
+
+
+def collect(x, axis, dim):
+    ways = lax.axis_size(axis)
+    up = [(d, (d + 1) % ways) for d in range(ways)]
+    down = [(d, (d - 1) % ways) for d in range(ways)]
+    earlier, later = ([x], [x])
+    for _ in range(ways // 2):
+        earlier.append(lax.ppermute(earlier[-1], axis, up))
+    for _ in range((ways - 1) // 2):
+        later.append(lax.ppermute(later[-1], axis, down))
+    line = jnp.concatenate([*earlier[::-1], *later[1:]], axis=dim)
+    return jnp.roll(line, (lax.axis_index(axis) - ways // 2) * x.shape[dim], axis=dim)
 
 
 def passed_along(x, axis, by):
@@ -46,7 +59,7 @@
         partial_value = jnp.take(face_stack, corners, axis=0).astype(jnp.float32)
         sector_total = lax.psum(partial_value.astype(jnp.bfloat16), "sub").astype(jnp.float32)
         sector_id = lax.axis_index("sector")
-        everything = lax.all_gather(sector_total, "sector", axis=0, tiled=True)
+        everything = collect(sector_total, "sector", 0)
         inverse_rows = lax.dynamic_slice_in_dim(
             coarse_inverse, sector_id * corner_count, corner_count, 0
         )

time: 301 us -> 319 us (1.060)
  waiting for transfers between devices: 18.6 us -> 35.2 us
  blocking collectives: 170 us -> 156 us
  starting transfers between devices: 18.8 us -> 29.7 us
    all_gather x2 -> x0, blocking collectives: 18.1 us -> none  [shards(): everything = lax.all_gather(sector_total, 'sector', axis=0, tiled=True)]
    ppermute x0 -> x14, waiting for transfers between devices: none -> 12.4 us  [the longest x8 6.52 us: collect(): earlier.append(lax.ppermute(earlier[-1], axis, up))]
    ppermute x0 -> x14, starting transfers between devices: none -> 10.6 us  [the longest x6 5.69 us: collect(): later.append(lax.ppermute(later[-1], axis, down))]
    psum x2, blocking collectives: 80.5 us -> 84 us  [squares(): lax.psum(jnp.sum(residual * residual, axis=(0, 1, 2, 3)), ('sector', 'sub'))]
  transfers between devices with their start and end apart: 8 -> 22, of which waited for: 4 -> 13; matrix products, arithmetic and copies ran while one was open for 21% -> 24% of each run, Pallas kernels for 0% -> 0%
where the time goes in v1:
time: 319 us; the launch traced here: 316 us
  blocking collectives  156 us (49%)
  local copies, waits for them, and re-layouts  57.4 us (18%)
  waiting for transfers between devices  35.2 us (11%)
  starting transfers between devices  29.7 us (9%)
  other arithmetic  21.2 us (7%)
  matrix products  14.9 us (5%)
    psum x2, blocking collectives, squares(): lax.psum(jnp.sum(residual * residual, axis=(0, 1, 2, 3)), ('sector', 'sub'))  84 us
    psum x1, blocking collectives, shards(): curvature = lax.psum(inner_sum(direction, image), ('sector', 'sub'))  43.5 us
    psum x2, blocking collectives, shards(): lax.psum(partial_value.astype(jnp.bfloat16), 'sub').astype(jnp.float32)  28.9 us
    gather x1, local copies, waits for them, and re-layouts, shards(): jnp.take(flexibility[0, 0], slot_order, axis=0)  20.8 us
    gather x1, local copies, waits for them, and re-layouts, shards(): jnp.take(jnp.take(flexibility[0, 0], slot_order, axis=0), slot_order, axi...  20.8 us
    ppermute x4, starting transfers between devices, passed_along(): return lax.ppermute(x, axis, pairs)  18.1 us
    ppermute x4, waiting for transfers between devices, passed_along(): return lax.ppermute(x, axis, pairs)  16.7 us
    dot_general x2, matrix products, shards(): jnp.dot(matrix, face_stack, preferred_element_type=jnp.float32) + correction  14.4 us
  transfers between devices with their start and end apart: 22, of which 13 were waited for; matrix products, arithmetic and copies ran while one was open for 24% of the time, Pallas kernels for 0%

profile of v1, /device:TPU:10, one launch (start us, length us, event | category | flops | bytes accessed | tf_op | source)
XLA Modules:
  0.0 316.1 jit_solution(9323652276445208473)
XLA Ops:
  2.1 3.5 %collective-permute-start = (bf16[512,256]{1,0:T(8,128)(2,1)S(1)}, bf16[512,256]{1,0:T(8,128)(2,1)S(1)}, u32[]{:S(2)}, u32[]{:S(2)}) collective-permute-start(bf16[512,256]{1,0:T(8,128)(2,1)S(1)} %get-tuple-element.28), channel_id=1, source_target_pairs={{0,1},{1,2},{2,3},{4,5},{5,6},{6,7},{8,9},{9,10},{10,11},{12,13},{... | collective-permute-start | bytes 786440 | tf_op jit(solution)/shard_map/ppermute | solution.py:25
  7.9 4.6 %collective-permute-done = bf16[512,256]{1,0:T(8,128)(2,1)S(1)} collective-permute-done((bf16[512,256]{1,0:T(8,128)(2,1)S(1)}, bf16[512,256]{1,0:T(8,128)(2,1)S(1)}, u32[]{:S(2)}, u32[]{:S(2)}) %collective-permute-start) | collective-permute-done | bytes 262176 | tf_op jit(solution)/shard_map/ppermute | solution.py:25
  13.4 15.4 %psum.43 = bf16[32,256]{1,0:T(8,128)(2,1)S(1)} all-reduce(bf16[32,256]{1,0:T(8,128)(2,1)S(1)} %broadcast_select_fusion.5), channel_id=1, replica_groups=mesh['sector'=8,'sub'=4] {'sub'}, use_global_device_ids=true, to_apply=%region_2.4 | all-reduce | flops 8192 | bytes 32768 | tf_op jit(solution)/shard_map/psum | solution.py:60
  28.9 20.8 %gather_fusion = bf16[2048,2048]{1,0:T(8,128)(2,1)} fusion(bf16[2048,2048]{1,0:T(8,128)(2,1)} %bitcast.49, s32[2048]{0:T(1024)S(1)} %broadcast_clamp_fusion), kind=kCustom, calls=%fused_computation.2 | custom fusion | bytes 16785408 | tf_op jit(solution)/shard_map/jit(_take)/gather | solution.py:46
  51.3 7.4 %broadcast_select_fusion = bf16[2048,2048]{1,0:T(8,128)(2,1)} fusion(bf16[2048,2048]{1,0:T(8,128)(2,1)} %gather_fusion, pred[2048]{0:T(1024)(128)(4,1)S(1)} %compare_and_fusion), kind=kLoop, calls=%fused_computation.6 | loop fusion | flops 4194304 | bytes 16779264 | tf_op jit(solution)/shard_map/jit(_take)/select_n | solution.py:46
  59.8 12.1 %copy.8 = bf16[2048,2048]{0,1:T(8,128)(2,1)} copy(bf16[2048,2048]{1,0:T(8,128)(2,1)} %broadcast_select_fusion) | data formatting | bytes 16777216 | tf_op jit(solution)/shard_map/jit(_take)/select_n | solution.py:46
  71.9 20.8 %gather_fusion.1 = bf16[2048,2048]{1,0:T(8,128)(2,1)} fusion(bf16[2048,2048]{0,1:T(8,128)(2,1)} %copy.8, s32[2048]{0:T(1024)S(1)} %broadcast_clamp_fusion), kind=kCustom, calls=%fused_computation.3 | custom fusion | bytes 16785408 | tf_op jit(solution)/shard_map/jit(_take)/gather | solution.py:46
  94.9 6.4 %fusion = f32[2048,256]{1,0:T(8,128)S(1)} fusion(bf16[2048,2048]{1,0:T(8,128)(2,1)} %gather_fusion.1, pred[2048]{0:T(1024)(128)(4,1)} %copy-done.9, bf16[512,256]{1,0:T(8,128)(2,1)S(1)} %get-tuple-element.29, bf16[512,256]{1,0:T(8,128)(2,1)S(1)} %neg.13, bf16[512,256]{1,0:T(8,128)(2,1)S(1)} %get-tuple-element.28, bf16[512,256]{1,0:T(8,128)(2,1)S(1)} %neg.12), kind=kOutput, calls=%fused_computation.8 | convolution fusion | flops 2155872256 | bytes 11536384 | tf_op jit(solution)/shard_map/dot_general | solution.py:74
  102.5 2.3 collective-permute-done.8
  108.1 6.1 %collective-permute-start.9 = (bf16[512,256]{1,0:T(8,128)(2,1)S(1)}, bf16[512,256]{1,0:T(8,128)(2,1)S(1)}, u32[]{:S(2)}, u32[]{:S(2)}) collective-permute-start(bf16[512,256]{1,0:T(8,128)(2,1)S(1)} %get-tuple-element.24), channel_id=1, source_target_pairs={{1,0},{2,1},{3,2},{5,4},{6,5},{7,6},{9,8},{10,9},{11,10},{13,12},{... | collective-permute-start | bytes 786440 | tf_op jit(solution)/shard_map/ppermute | solution.py:25
  115.0 3.4 %collective-permute-done.9 = bf16[512,256]{1,0:T(8,128)(2,1)S(1)} collective-permute-done((bf16[512,256]{1,0:T(8,128)(2,1)S(1)}, bf16[512,256]{1,0:T(8,128)(2,1)S(1)}, u32[]{:S(2)}, u32[]{:S(2)}) %collective-permute-start.9) | collective-permute-done | bytes 262176 | tf_op jit(solution)/shard_map/ppermute | solution.py:25
  120.5 43.4 %all-reduce = (f32[256]{0:T(256)S(1)}, f32[256]{0:T(256)S(1)}) all-reduce(f32[256]{0:T(256)S(1)} %get-tuple-element.5, f32[256]{0:T(256)S(1)} %get-tuple-element.4), channel_id=1, replica_groups=mesh['sector'=8,'sub'=4] {'sector','sub'}, use_global_device_ids=true, to_apply=%region_1.2 | all-reduce | flops 512 | bytes 4096 | tf_op jit(solution)/shard_map/psum | solution.py:35
  164.1 40.6 %psum.45 = f32[256]{0:T(256)S(1)} all-reduce(f32[256]{0:T(256)S(1)} %multiply_reduce_fusion), channel_id=1, replica_groups=mesh['sector'=8,'sub'=4] {'sector','sub'}, use_global_device_ids=true, to_apply=%region_7.10 | all-reduce | flops 256 | bytes 2048 | tf_op jit(solution)/shard_map/psum | solution.py:35
  205.1 2.6 collective-permute-start.11
  207.7 3.2 %collective-permute-done.12 = bf16[512,256]{1,0:T(8,128)(2,1)S(1)} collective-permute-done((bf16[512,256]{1,0:T(8,128)(2,1)S(1)}, bf16[512,256]{1,0:T(8,128)(2,1)S(1)}, u32[]{:S(2)}, u32[]{:S(2)}) %collective-permute-start.12) | collective-permute-done | bytes 262176 | tf_op jit(solution)/shard_map/ppermute | solution.py:31
  211.0 4.7 %collective-permute-done.11 = bf16[512,256]{1,0:T(8,128)(2,1)S(1)} collective-permute-done((bf16[512,256]{1,0:T(8,128)(2,1)S(1)}, bf16[512,256]{1,0:T(8,128)(2,1)S(1)}, u32[]{:S(2)}, u32[]{:S(2)}) %collective-permute-start.11) | collective-permute-done | bytes 262176 | tf_op jit(solution)/shard_map/ppermute | solution.py:25
  217.3 13.6 %psum.46 = bf16[32,256]{1,0:T(8,128)(2,1)S(1)} all-reduce(bf16[32,256]{1,0:T(8,128)(2,1)S(1)} %broadcast_select_fusion.4), channel_id=1, replica_groups=mesh['sector'=8,'sub'=4] {'sub'}, use_global_device_ids=true, to_apply=%region_8.11 | all-reduce | flops 8192 | bytes 32768 | tf_op jit(solution)/shard_map/psum | solution.py:60
  231.0 3.3 %collective-permute-done.13 = f32[32,256]{1,0:T(8,128)S(1)} collective-permute-done((f32[32,256]{1,0:T(8,128)S(1)}, f32[32,256]{1,0:T(8,128)S(1)}, u32[]{:S(2)}, u32[]{:S(2)}) %collective-permute-start.13) | collective-permute-done | bytes 32800 | tf_op jit(solution)/shard_map/ppermute | solution.py:15
  242.5 7.9 %fusion.1 = f32[2048,256]{1,0:T(8,128)} fusion(bf16[2048,2048]{1,0:T(8,128)(2,1)} %gather_fusion.1, pred[2048]{0:T(1024)(128)(4,1)S(1)} %copy-done.10, bf16[512,256]{1,0:T(8,128)(2,1)} %copy-done.7, bf16[512,256]{1,0:T(8,128)(2,1)} %copy-done.4, bf16[512,256]{1,0:T(8,128)(2,1)} %copy-done.6, bf16[512,256]{1,0:T(8,128)(2,1)} %copy-done.5), kind=kOutput, calls=%fused_computation.9 | convolution fusion | flops 2155872256 | bytes 11536384 | tf_op jit(solution)/shard_map/dot_general | solution.py:74
  250.8 3.6 %collective-permute-done.19 = f32[32,256]{1,0:T(8,128)S(1)} collective-permute-done((f32[32,256]{1,0:T(8,128)S(1)}, f32[32,256]{1,0:T(8,128)S(1)}, u32[]{:S(2)}, u32[]{:S(2)}) %collective-permute-start.19) | collective-permute-done | bytes 32800 | tf_op jit(solution)/shard_map/ppermute | solution.py:17
  254.6 3.7 %scatter_fusion.1 = f32[2048,256]{1,0:T(8,128)} fusion(f32[2048,256]{1,0:T(8,128)} %fusion.1, s32[32]{0:T(128)S(1)} %copy-done.12, f32[32,256]{1,0:T(8,128)S(1)} %convolution_multiply_fusion), kind=kCustom, calls=%fused_computation.5 | custom fusion | flops 8192 | bytes 98432 | tf_op jit(solution)/shard_map/scatter-add | solution.py:73
  260.2 6.0 %collective-permute-start.20 = (bf16[512,256]{1,0:T(8,128)(2,1)S(1)}, bf16[512,256]{1,0:T(8,128)(2,1)S(1)}, u32[]{:S(2)}, u32[]{:S(2)}) collective-permute-start(bf16[512,256]{1,0:T(8,128)(2,1)S(1)} %get-tuple-element.22), channel_id=1, source_target_pairs={{1,0},{2,1},{3,2},{5,4},{6,5},{7,6},{9,8},{10,9},{11,10},{13,12},{... | collective-permute-start | bytes 786440 | tf_op jit(solution)/shard_map/ppermute | solution.py:25
  266.3 4.0 %collective-permute-done.20 = bf16[512,256]{1,0:T(8,128)(2,1)S(1)} collective-permute-done((bf16[512,256]{1,0:T(8,128)(2,1)S(1)}, bf16[512,256]{1,0:T(8,128)(2,1)S(1)}, u32[]{:S(2)}, u32[]{:S(2)}) %collective-permute-start.20) | collective-permute-done | bytes 262176 | tf_op jit(solution)/shard_map/ppermute | solution.py:25
  270.9 43.5 %psum.47 = f32[256]{0:T(256)S(1)} all-reduce(f32[256]{0:T(256)S(1)} %fusion.6), channel_id=1, replica_groups=mesh['sector'=8,'sub'=4] {'sector','sub'}, use_global_device_ids=true, to_apply=%region_11.14 | all-reduce | flops 256 | bytes 2048 | tf_op jit(solution)/shard_map/psum | solution.py:86
  (119 shorter events, 32.0 us)
Async XLA Ops:
  0.6 104.1 %copy-start = (f32[256,256]{1,0:T(8,128)S(1)}, f32[256,256]{1,0:T(8,128)}, u32[]{:S(2)}) copy-start(f32[256,256]{1,0:T(8,128)} %param.13) | copy-start | bytes 786436
  2.0 5.8 %collective-permute-start.1 = (bf16[512,256]{1,0:T(8,128)(2,1)S(1)}, bf16[512,256]{1,0:T(8,128)(2,1)S(1)}, u32[]{:S(2)}, u32[]{:S(2)}) collective-permute-start(bf16[512,256]{1,0:T(8,128)(2,1)S(1)} %get-tuple-element.29), channel_id=1, source_target_pairs={{0,4},{4,8},{8,12},{12,16},{16,20},{20,24},{24,28},{28,0},{1,5},{5... | collective-permute-start | bytes 786440 | tf_op jit(solution)/shard_map/ppermute | solution.py:31
  2.1 10.5 %collective-permute-start = (bf16[512,256]{1,0:T(8,128)(2,1)S(1)}, bf16[512,256]{1,0:T(8,128)(2,1)S(1)}, u32[]{:S(2)}, u32[]{:S(2)}) collective-permute-start(bf16[512,256]{1,0:T(8,128)(2,1)S(1)} %get-tuple-element.28), channel_id=1, source_target_pairs={{0,1},{1,2},{2,3},{4,5},{5,6},{6,7},{8,9},{9,10},{10,11},{12,13},{... | collective-permute-start | bytes 786440 | tf_op jit(solution)/shard_map/ppermute | solution.py:25
  5.6 44.0 %copy-start.13 = (pred[32]{0:T(512)(128)(4,1)}, pred[32]{0:T(512)(128)(4,1)S(1)}, u32[]{:S(2)}) copy-start(pred[32]{0:T(512)(128)(4,1)S(1)} %compare_and_fusion.1) | copy-start | bytes 100
  28.8 20.9 %collective-permute-start.2 = (f32[32,256]{1,0:T(8,128)S(1)}, f32[32,256]{1,0:T(8,128)S(1)}, u32[]{:S(2)}, u32[]{:S(2)}) collective-permute-start(f32[32,256]{1,0:T(8,128)S(1)} %convert_element_type.35), channel_id=1, source_target_pairs={{0,4},{4,8},{8,12},{12,16},{16,20},{20,24},{24,28},{28,0},{1,5},{5... | collective-permute-start | bytes 98312 | tf_op jit(solution)/shard_map/ppermute | solution.py:15
  49.7 9.2 %collective-permute-start.3 = (f32[32,256]{1,0:T(8,128)S(1)}, f32[32,256]{1,0:T(8,128)S(1)}, u32[]{:S(2)}, u32[]{:S(2)}) collective-permute-start(f32[32,256]{1,0:T(8,128)S(1)} %collective-permute-done.2), channel_id=1, source_target_pairs={{0,4},{4,8},{8,12},{12,16},{16,20},{20,24},{24,28},{28,0},{1,5},{5... | collective-permute-start | bytes 98312 | tf_op jit(solution)/shard_map/ppermute | solution.py:15
  58.7 34.0 %collective-permute-start.6 = (f32[32,256]{1,0:T(8,128)S(1)}, f32[32,256]{1,0:T(8,128)S(1)}, u32[]{:S(2)}, u32[]{:S(2)}) collective-permute-start(f32[32,256]{1,0:T(8,128)S(1)} %convert_element_type.35), channel_id=1, source_target_pairs={{0,28},{4,0},{8,4},{12,8},{16,12},{20,16},{24,20},{28,24},{1,29},{... | collective-permute-start | bytes 98312 | tf_op jit(solution)/shard_map/ppermute | solution.py:17
  58.9 35.3 %collective-permute-start.4 = (f32[32,256]{1,0:T(8,128)S(1)}, f32[32,256]{1,0:T(8,128)S(1)}, u32[]{:S(2)}, u32[]{:S(2)}) collective-permute-start(f32[32,256]{1,0:T(8,128)S(1)} %collective-permute-done.3), channel_id=1, source_target_pairs={{0,4},{4,8},{8,12},{12,16},{16,20},{20,24},{24,28},{28,0},{1,5},{5... | collective-permute-start | bytes 98312 | tf_op jit(solution)/shard_map/ppermute | solution.py:15
  92.7 8.7 %collective-permute-start.7 = (f32[32,256]{1,0:T(8,128)S(1)}, f32[32,256]{1,0:T(8,128)S(1)}, u32[]{:S(2)}, u32[]{:S(2)}) collective-permute-start(f32[32,256]{1,0:T(8,128)S(1)} %collective-permute-done.6), channel_id=1, source_target_pairs={{0,28},{4,0},{8,4},{12,8},{16,12},{20,16},{24,20},{28,24},{1,29},{... | collective-permute-start | bytes 98312 | tf_op jit(solution)/shard_map/ppermute | solution.py:17
  94.1 8.3 %collective-permute-start.5 = (f32[32,256]{1,0:T(8,128)S(1)}, f32[32,256]{1,0:T(8,128)S(1)}, u32[]{:S(2)}, u32[]{:S(2)}) collective-permute-start(f32[32,256]{1,0:T(8,128)S(1)} %collective-permute-done.4), channel_id=1, source_target_pairs={{0,4},{4,8},{8,12},{12,16},{16,20},{20,24},{24,28},{28,0},{1,5},{5... | collective-permute-start | bytes 98312 | tf_op jit(solution)/shard_map/ppermute | solution.py:15
  101.4 3.3 %collective-permute-start.8 = (f32[32,256]{1,0:T(8,128)S(1)}, f32[32,256]{1,0:T(8,128)S(1)}, u32[]{:S(2)}, u32[]{:S(2)}) collective-permute-start(f32[32,256]{1,0:T(8,128)S(1)} %collective-permute-done.7), channel_id=1, source_target_pairs={{0,28},{4,0},{8,4},{12,8},{16,12},{20,16},{24,20},{28,24},{1,29},{... | collective-permute-start | bytes 98312 | tf_op jit(solution)/shard_map/ppermute | solution.py:17
  108.1 10.2 %collective-permute-start.9 = (bf16[512,256]{1,0:T(8,128)(2,1)S(1)}, bf16[512,256]{1,0:T(8,128)(2,1)S(1)}, u32[]{:S(2)}, u32[]{:S(2)}) collective-permute-start(bf16[512,256]{1,0:T(8,128)(2,1)S(1)} %get-tuple-element.24), channel_id=1, source_target_pairs={{1,0},{2,1},{3,2},{5,4},{6,5},{7,6},{9,8},{10,9},{11,10},{13,12},{... | collective-permute-start | bytes 786440 | tf_op jit(solution)/shard_map/ppermute | solution.py:25
  114.3 4.6 %collective-permute-start.10 = (bf16[512,256]{1,0:T(8,128)(2,1)S(1)}, bf16[512,256]{1,0:T(8,128)(2,1)S(1)}, u32[]{:S(2)}, u32[]{:S(2)}) collective-permute-start(bf16[512,256]{1,0:T(8,128)(2,1)S(1)} %get-tuple-element.25), channel_id=1, source_target_pairs={{0,28},{4,0},{8,4},{12,8},{16,12},{20,16},{24,20},{28,24},{1,29},{... | collective-permute-start | bytes 786440 | tf_op jit(solution)/shard_map/ppermute | solution.py:31
  205.1 5.8 %collective-permute-start.12 = (bf16[512,256]{1,0:T(8,128)(2,1)S(1)}, bf16[512,256]{1,0:T(8,128)(2,1)S(1)}, u32[]{:S(2)}, u32[]{:S(2)}) collective-permute-start(bf16[512,256]{1,0:T(8,128)(2,1)S(1)} %get-tuple-element.27), channel_id=1, source_target_pairs={{0,4},{4,8},{8,12},{12,16},{16,20},{20,24},{24,28},{28,0},{1,5},{5... | collective-permute-start | bytes 786440 | tf_op jit(solution)/shard_map/ppermute | solution.py:31
  205.1 10.5 %collective-permute-start.11 = (bf16[512,256]{1,0:T(8,128)(2,1)S(1)}, bf16[512,256]{1,0:T(8,128)(2,1)S(1)}, u32[]{:S(2)}, u32[]{:S(2)}) collective-permute-start(bf16[512,256]{1,0:T(8,128)(2,1)S(1)} %get-tuple-element.26), channel_id=1, source_target_pairs={{0,1},{1,2},{2,3},{4,5},{5,6},{6,7},{8,9},{9,10},{10,11},{12,13},{... | collective-permute-start | bytes 786440 | tf_op jit(solution)/shard_map/ppermute | solution.py:25
  230.9 3.4 %collective-permute-start.13 = (f32[32,256]{1,0:T(8,128)S(1)}, f32[32,256]{1,0:T(8,128)S(1)}, u32[]{:S(2)}, u32[]{:S(2)}) collective-permute-start(f32[32,256]{1,0:T(8,128)S(1)} %convert_element_type.39), channel_id=1, source_target_pairs={{0,4},{4,8},{8,12},{12,16},{16,20},{20,24},{24,28},{28,0},{1,5},{5... | collective-permute-start | bytes 98312 | tf_op jit(solution)/shard_map/ppermute | solution.py:15
  234.3 3.3 %collective-permute-start.14 = (f32[32,256]{1,0:T(8,128)S(1)}, f32[32,256]{1,0:T(8,128)S(1)}, u32[]{:S(2)}, u32[]{:S(2)}) collective-permute-start(f32[32,256]{1,0:T(8,128)S(1)} %collective-permute-done.13), channel_id=1, source_target_pairs={{0,4},{4,8},{8,12},{12,16},{16,20},{20,24},{24,28},{28,0},{1,5},{5... | collective-permute-start | bytes 98312 | tf_op jit(solution)/shard_map/ppermute | solution.py:15
  234.3 3.9 %collective-permute-start.17 = (f32[32,256]{1,0:T(8,128)S(1)}, f32[32,256]{1,0:T(8,128)S(1)}, u32[]{:S(2)}, u32[]{:S(2)}) collective-permute-start(f32[32,256]{1,0:T(8,128)S(1)} %convert_element_type.39), channel_id=1, source_target_pairs={{0,28},{4,0},{8,4},{12,8},{16,12},{20,16},{24,20},{28,24},{1,29},{... | collective-permute-start | bytes 98312 | tf_op jit(solution)/shard_map/ppermute | solution.py:17
  237.6 3.3 %collective-permute-start.15 = (f32[32,256]{1,0:T(8,128)S(1)}, f32[32,256]{1,0:T(8,128)S(1)}, u32[]{:S(2)}, u32[]{:S(2)}) collective-permute-start(f32[32,256]{1,0:T(8,128)S(1)} %collective-permute-done.14), channel_id=1, source_target_pairs={{0,4},{4,8},{8,12},{12,16},{16,20},{20,24},{24,28},{28,0},{1,5},{5... | collective-permute-start | bytes 98312 | tf_op jit(solution)/shard_map/ppermute | solution.py:15
  238.2 12.2 %collective-permute-start.18 = (f32[32,256]{1,0:T(8,128)S(1)}, f32[32,256]{1,0:T(8,128)S(1)}, u32[]{:S(2)}, u32[]{:S(2)}) collective-permute-start(f32[32,256]{1,0:T(8,128)S(1)} %collective-permute-done.17), channel_id=1, source_target_pairs={{0,28},{4,0},{8,4},{12,8},{16,12},{20,16},{24,20},{28,24},{1,29},{... | collective-permute-start | bytes 98312 | tf_op jit(solution)/shard_map/ppermute | solution.py:17
  241.0 9.7 %collective-permute-start.16 = (f32[32,256]{1,0:T(8,128)S(1)}, f32[32,256]{1,0:T(8,128)S(1)}, u32[]{:S(2)}, u32[]{:S(2)}) collective-permute-start(f32[32,256]{1,0:T(8,128)S(1)} %collective-permute-done.15), channel_id=1, source_target_pairs={{0,4},{4,8},{8,12},{12,16},{16,20},{20,24},{24,28},{28,0},{1,5},{5... | collective-permute-start | bytes 98312 | tf_op jit(solution)/shard_map/ppermute | solution.py:15
  250.4 3.9 %collective-permute-start.19 = (f32[32,256]{1,0:T(8,128)S(1)}, f32[32,256]{1,0:T(8,128)S(1)}, u32[]{:S(2)}, u32[]{:S(2)}) collective-permute-start(f32[32,256]{1,0:T(8,128)S(1)} %collective-permute-done.18), channel_id=1, source_target_pairs={{0,28},{4,0},{8,4},{12,8},{16,12},{20,16},{24,20},{28,24},{1,29},{... | collective-permute-start | bytes 98312 | tf_op jit(solution)/shard_map/ppermute | solution.py:17
  260.2 10.1 %collective-permute-start.20 = (bf16[512,256]{1,0:T(8,128)(2,1)S(1)}, bf16[512,256]{1,0:T(8,128)(2,1)S(1)}, u32[]{:S(2)}, u32[]{:S(2)}) collective-permute-start(bf16[512,256]{1,0:T(8,128)(2,1)S(1)} %get-tuple-element.22), channel_id=1, source_target_pairs={{1,0},{2,1},{3,2},{5,4},{6,5},{7,6},{9,8},{10,9},{11,10},{13,12},{... | collective-permute-start | bytes 786440 | tf_op jit(solution)/shard_map/ppermute | solution.py:25
  266.2 4.3 %collective-permute-start.21 = (bf16[512,256]{1,0:T(8,128)(2,1)S(1)}, bf16[512,256]{1,0:T(8,128)(2,1)S(1)}, u32[]{:S(2)}, u32[]{:S(2)}) collective-permute-start(bf16[512,256]{1,0:T(8,128)(2,1)S(1)} %get-tuple-element.23), channel_id=1, source_target_pairs={{0,28},{4,0},{8,4},{12,8},{16,12},{20,16},{24,20},{28,24},{1,29},{... | collective-permute-start | bytes 786440 | tf_op jit(solution)/shard_map/ppermute | solution.py:31
  (14 other events, 165.3 us)
